TPU v7x, 32 devices: a whole 2x2x4 slice. The times are simulated.
32 devices in a mesh: grp: 8 (over z, x), rep: 4 (over y, core).
Axes of the slice: x: 2, y: 2, z: 4, core: 2. Of those that a mesh axis runs over, the one named last changes fastest.
Arguments:
- three_center: bfloat16 [4, 64, 32, 6, 4096], P('rep', 'grp'), may hold values from -2 to 2
- metric: bfloat16 [4, 64, 64], P('rep'), may hold values from -0.75 to 0.75
- occupied: bfloat16 [2048, 48], replicated, may hold values from -0.3125 to 0.3125
- nu_list: int32 [32, 6], replicated, may hold values from 0 to 31, as said below
- nu_count: int32 [32], replicated, may hold values from 1 to 6
- block_size: int32 [32], replicated, may hold values from 32 to 64
Outputs:
- exchange_matrix: float32 [2048, 2048], P('rep', 'grp')
Inputs may be any that keep to these rules, and one draw needn't show every extreme that they name: `nu_list`: entry 0 of row m is m itself; the other entries of a row are distinct blocks other than m.
All inputs are finite; a program needn't handle non-finite values.
Results may differ from a plain program's by a relative error of at most 0.0024.
Values may be sent and summed in bfloat16 or wider, within the bound.
No kernel may reach another device: no remote copies, remote signals or barrier semaphores. Data moves between devices by JAX's collectives and lax.ppermute only.
A program may use at most 192 MiB of HBM per device.

v0:
```python
import jax
import jax.numpy as jnp
from jax import lax
from jax.sharding import PartitionSpec as P

NB = 64


def body(three_center, metric, occupied, nu_list, nu_count, block_size):
    n_mu, knu = nu_list.shape
    n_occ = occupied.shape[1]
    aux_dev = three_center.shape[1]
    lanes = jnp.arange(NB, dtype=jnp.int32)
    row_live = lanes[None, :] < block_size[:, None]
    col_live = lanes[None, None, :] < block_size[nu_list][:, :, None]
    slot_live = jnp.arange(knu, dtype=jnp.int32)[None, :] < nu_count[:, None]
    mask = row_live[:, None, :, None] & col_live[:, :, None, :] & slot_live[:, :, None, None]
    blocks = three_center[0].reshape(aux_dev, n_mu, knu, NB, NB)
    masked = jnp.where(mask[None], blocks, jnp.zeros((), jnp.bfloat16))
    picked = occupied.reshape(n_mu, NB, n_occ)[nu_list]
    half = jnp.einsum(
        "qmkab,mkbi->qmai", masked, picked, preferred_element_type=jnp.float32
    ).astype(jnp.bfloat16)
    half = half.reshape(aux_dev, n_mu, NB * n_occ)
    regrouped = lax.all_to_all(half, "grp", split_axis=1, concat_axis=0, tiled=True)
    n_aux = regrouped.shape[0]
    mu_dev = regrouped.shape[1]
    regrouped = regrouped.reshape(n_aux, mu_dev, NB, n_occ)
    orbital = jnp.einsum(
        "pq,qmai->mapi", metric[0], regrouped, preferred_element_type=jnp.float32
    ).astype(jnp.bfloat16)
    orbital = orbital.reshape(mu_dev * NB, n_aux * n_occ)
    term = jnp.dot(
        lax.all_gather(orbital, "grp", axis=0, tiled=True),
        orbital.T,
        preferred_element_type=jnp.float32,
    )
    return lax.psum_scatter(term, "rep", scatter_dimension=0, tiled=True)


def solution(mesh):
    return jax.shard_map(
        body,
        mesh=mesh,
        in_specs=(P("rep", "grp", None, None, None), P("rep", None, None), P(), P(), P(), P()),
        out_specs=P("rep", "grp"),
        check_vma=False,
    )
```

profile of v0, /device:TPU:0, one launch (start us, length us, event | category | flops | bytes accessed | tf_op | source)
XLA Modules:
  0.0 370.5 jit_solution(7674496762199158850)
XLA Ops:
  6.5 0.0 copy-start
  6.5 0.0 copy-start.1
  6.5 0.0 all-gather.2.cloned.1.call-start
  6.5 0.7 compare_select_fusion
  7.3 0.7 iota_compare_fusion.1
  8.0 0.7 iota_compare_fusion.2
  8.7 0.1 copy.22
  8.8 0.1 reshape.66
  8.9 0.0 copy-done.1
  8.9 0.0 copy-start.2
  8.9 1.6 gather_fusion.1
  10.5 0.1 reshape.73
  10.6 0.1 iota_compare_fusion
  10.7 0.0 copy-done.2
  10.7 0.4 reshape.60
  11.1 0.2 copy.23
  11.3 1.0 gather_fusion
  12.3 34.4 %reshape_squeeze.3 = bf16[8,32,6,64,64]{4,3,1,2,0:T(8,128)(2,1)} reshape(bf16[1,8,32,6,4096]{4,2,3,1,0:T(8,128)(2,1)} %param.6) | data formatting | bytes 25165824 | tf_op jit(solution)/shard_map/reshape;squeeze | solution.py:18
  46.7 2.3 and_and_fusion
  49.0 17.0 %fusion.3 = bf16[8,32,64,48]{2,3,0,1:T(8,128)(2,1)} fusion(bf16[32,6,64,48,1]{2,3,1,4,0:T(8,128)(2,1)S(1)} %bitcast.47, bf16[8,32,6,64,64]{4,3,1,2,0:T(8,128)(2,1)} %reshape_squeeze.3, pred[32,6,64,64]{3,2,1,0:T(8,128)(4,1)} %and_and_fusion), kind=kOutput, calls=%fused_computation.8 | convolution fusion | flops 611057664 | bytes 16121856 | tf_op jit(solution)/shard_map/qmkab,mkbi->qmai/dot_general | solution.py:21
  66.0 6.2 %copy.33 = bf16[8,32,64,48]{3,2,0,1:T(8,128)(2,1)} copy(bf16[8,32,64,48]{2,3,0,1:T(8,128)(2,1)} %fusion.3) | data formatting | bytes 3145728 | tf_op jit(solution)/shard_map/reshape | solution.py:24
  72.2 8.0 %reshape.87 = bf16[8,32,3072]{2,0,1:T(8,128)(2,1)S(1)} reshape(bf16[8,32,64,48]{3,2,0,1:T(8,128)(2,1)} %copy.33) | data formatting | bytes 3145728 | tf_op jit(solution)/shard_map/reshape | solution.py:24
  80.2 44.1 %all_to_all.15 = bf16[8,32,3072]{2,0,1:T(8,128)(2,1)S(1)} all-to-all(bf16[8,32,3072]{2,0,1:T(8,128)(2,1)S(1)} %reshape.87), channel_id=1, replica_groups=mesh['grp'=8,'rep'=4] {'grp'}, dimensions={1} | all-to-all | bytes 3145728 | tf_op jit(solution)/shard_map/all_to_all | solution.py:25
  124.2 0.1 copy.40
  124.3 5.3 %reshape.62 = bf16[64,4,64,48]{3,2,0,1:T(8,128)(2,1)} reshape(bf16[8,8,4,3072]{3,1,0,2:T(8,128)(2,1)S(1)} %bitcast.46) | data formatting | bytes 3145728 | tf_op jit(solution)/shard_map/reshape | solution.py:28
  129.7 6.4 %copy.28 = bf16[64,4,64,48]{0,2,3,1:T(8,128)(2,1)S(1)} copy(bf16[64,4,64,48]{3,2,0,1:T(8,128)(2,1)} %reshape.62) | data formatting | bytes 3145728 | tf_op jit(solution)/shard_map/reshape | solution.py:28
  136.1 0.0 copy-done
  136.1 2.6 convert_bitcast_fusion
  138.7 6.3 %copy.29 = bf16[4,64,64,48]{1,0,3,2:T(4,128)(2,1)S(1)} copy(bf16[4,64,64,48]{2,1,3,0:T(8,128)(2,1)} %convert_bitcast_fusion) | data formatting | bytes 3145728 | tf_op jit(solution)/shard_map/convert_element_type | solution.py:31
  145.1 3.0 reshape.63
  148.1 0.0 all-gather.2.cloned.1.call-update
  148.1 0.0 reduce-scatter.2.cloned.1.call-start
  148.2 175.7 %all-gather.2.cloned.1.call-done = bf16[2048,3072]{0,1:T(8,128)(2,1)} async-done(((bf16[256,3072]{0,1:T(8,128)(2,1)}), bf16[2048,3072]{0,1:T(8,128)(2,1)}) %all-gather.2.cloned.1.call-update) | async-done | bytes 12582928 | tf_op jit(solution)/shard_map/all_gather | solution.py:34
  323.9 10.0 %fusion.6 = f32[2048,256]{1,0:T(8,128)} fusion(bf16[2048,3072]{0,1:T(8,128)(2,1)} %all-gather.2.cloned.1.call-done, bf16[256,3072]{0,1:T(8,128)(2,1)} %reshape.63), kind=kOutput, calls=%fused_computation.18 | convolution fusion | flops 3221225472 | bytes 16252928 | tf_op jit(solution)/shard_map/dot_general | solution.py:33
  333.9 0.0 reduce-scatter.2.cloned.1.call-update
  333.9 29.8 %reduce-scatter.2.cloned.1.call-done = f32[512,256]{1,0:T(8,128)} async-done(((f32[2048,256]{1,0:T(8,128)}), f32[512,256]{1,0:T(8,128)}) %reduce-scatter.2.cloned.1.call-update) | async-done | bytes 524304 | tf_op jit(solution)/shard_map/reduce_scatter | solution.py:38
  (1 shorter events, 0.0 us)
Async XLA Ops:
  6.5 129.6 %copy-start = (bf16[1,64,64]{2,1,0:T(8,128)(2,1)S(1)}, bf16[1,64,64]{2,1,0:T(8,128)(2,1)}, u32[]{:S(2)}) copy-start(bf16[1,64,64]{2,1,0:T(8,128)(2,1)} %param.7) | copy-start | bytes 24580
  6.5 2.4 copy-start.1
  6.5 317.3 %all-gather.2.cloned.1.call-start = ((), (), s32[]{:S(2)}) async-start(), calls=%async_computation.2 | async-start | bytes 14155776 | tf_op jit(solution)/shard_map/all_gather | solution.py:34
  8.9 1.8 copy-start.2
  148.1 215.5 %reduce-scatter.2.cloned.1.call-start = ((), (), s32[]{:S(2)}) async-start(), calls=%async_computation.3 | async-start | bytes 2621440 | tf_op jit(solution)/shard_map/reduce_scatter | solution.py:38
Sparse Core Ops, SparseCore 0:
  148.2 175.5 all-gather.1
  334.0 29.5 reduce-scatter.1
where the time goes:
time: 372 us; the launch traced here: 370 us
  waiting for transfers between devices  205 us (55%)
  local copies, waits for them, and re-layouts  73.1 us (20%)
  blocking collectives  44.1 us (12%)
  matrix products  29.6 us (8%)
  between operations  13.5 us (4%)
  other arithmetic  4.59 us (1%)
    all_gather x1, waiting for transfers between devices, body(): lax.all_gather(orbital, 'grp', axis=0, tiled=True)  176 us
    all_to_all x1, blocking collectives, body(): lax.all_to_all(half, 'grp', split_axis=1, concat_axis=0, tiled=True)  44.1 us
    another operation x1, local copies, waits for them, and re-layouts, body(): blocks = three_center[0].reshape(aux_dev, n_mu, knu, NB, NB)  34.4 us
    reduce_scatter x1, waiting for transfers between devices, body(): return lax.psum_scatter(term, 'rep', scatter_dimension=0, tiled=True)  29.8 us
    dot_general x1, matrix products, body(): jnp.einsum('qmkab,mkbi->qmai', masked, picked, preferred_element_type=jnp...  17 us
    reshape x2, local copies, waits for them, and re-layouts, body(): half = half.reshape(aux_dev, n_mu, NB * n_occ)  14.1 us
    reshape x2, local copies, waits for them, and re-layouts, body(): regrouped = regrouped.reshape(n_aux, mu_dev, NB, n_occ)  11.8 us
    dot_general x1, matrix products, body(): jnp.dot(lax.all_gather(orbital, 'grp', axis=0, tiled=True), orbital.T, pr...  9.99 us
  transfers between devices with their start and end apart: 2, of which 2 were waited for; matrix products, arithmetic and copies ran while one was open for 0% of the time, Pallas kernels for 0%

commit v1 on v0

--- a/solution.py
+++ b/solution.py
@@ -4,6 +4,23 @@
 from jax.sharding import PartitionSpec as P
 
 NB = 64
+
+
+def take_classes_for(v0, net_axis):
+    mat_out, long_array, main = (
+        jax.lax.axis_size(net_axis),
+        jax.lax.axis_index(net_axis),
+        v0.shape[0],
+    )
+    tile_out, lower = (v0, 1)
+    while lower < mat_out:
+        seen = []
+        for b in range(mat_out):
+            seen.append((b, (b - lower) % mat_out))
+        tile_out = jnp.concatenate([tile_out, jax.lax.ppermute(tile_out, net_axis, seen)], axis=0)
+        lower = 2 * lower
+    inter = jnp.roll(tile_out, long_array * main, axis=0)
+    return inter
 
 
 def body(three_center, metric, occupied, nu_list, nu_count, block_size):
@@ -30,11 +47,7 @@
         "pq,qmai->mapi", metric[0], regrouped, preferred_element_type=jnp.float32
     ).astype(jnp.bfloat16)
     orbital = orbital.reshape(mu_dev * NB, n_aux * n_occ)
-    term = jnp.dot(
-        lax.all_gather(orbital, "grp", axis=0, tiled=True),
-        orbital.T,
-        preferred_element_type=jnp.float32,
-    )
+    term = jnp.dot(take_classes_for(orbital, "grp"), orbital.T, preferred_element_type=jnp.float32)
     return lax.psum_scatter(term, "rep", scatter_dimension=0, tiled=True)
 
 

time: 372 us -> 597 us (1.60)
  waiting for transfers between devices: 205 us -> 400 us
  local copies, waits for them, and re-layouts: 73.1 us -> 98.4 us
    ppermute x0 -> x3, waiting for transfers between devices: none -> 367 us  [take_classes_for(): jax.lax.ppermute(tile_out, net_axis, seen)]
    all_gather x1 -> x0, waiting for transfers between devices: 176 us -> none  [body(): lax.all_gather(orbital, 'grp', axis=0, tiled=True)]
    unnamed x6 -> x17, local copies, waits for them, and re-layouts: 0.01 us -> 15.4 us
    concatenate x0 -> x1, local copies, waits for them, and re-layouts: none -> 6.15 us  [take_classes_for(): inter = jnp.roll(tile_out, long_array * main, axis=0)]
  transfers between devices with their start and end apart: 2 -> 4, of which waited for: 2 -> 4; matrix products, arithmetic and copies ran while one was open for 0% -> 1% of each run, Pallas kernels for 0% -> 0%
where the time goes in v1:
time: 597 us; the launch traced here: 596 us
  waiting for transfers between devices  400 us (67%)
  local copies, waits for them, and re-layouts  98.4 us (16%)
  blocking collectives  44.1 us (7%)
  matrix products  27.6 us (5%)
  between operations  13.5 us (2%)
  other arithmetic  7.76 us (1%)
    ppermute x3, waiting for transfers between devices, take_classes_for(): jax.lax.ppermute(tile_out, net_axis, seen)  367 us
    all_to_all x1, blocking collectives, body(): lax.all_to_all(half, 'grp', split_axis=1, concat_axis=0, tiled=True)  44.1 us
    another operation x1, local copies, waits for them, and re-layouts, body(): blocks = three_center[0].reshape(aux_dev, n_mu, knu, NB, NB)  34.4 us
    reduce_scatter x1, waiting for transfers between devices, body(): return lax.psum_scatter(term, 'rep', scatter_dimension=0, tiled=True)  33.5 us
    dot_general x1, matrix products, body(): jnp.einsum('qmkab,mkbi->qmai', masked, picked, preferred_element_type=jnp...  17 us
    unnamed x17, local copies, waits for them, and re-layouts  15.4 us
    reshape x2, local copies, waits for them, and re-layouts, body(): half = half.reshape(aux_dev, n_mu, NB * n_occ)  14.1 us
  transfers between devices with their start and end apart: 4, of which 4 were waited for; matrix products, arithmetic and copies ran while one was open for 1% of the time, Pallas kernels for 0%

profile of v1, /device:TPU:0, one launch (start us, length us, event | category | flops | bytes accessed | tf_op | source)
XLA Modules:
  0.0 595.6 jit_solution(8123244254941862198)
XLA Ops:
  6.5 0.0 copy-start
  6.5 0.0 copy-start.1
  6.5 0.0 reduce-scatter.2.cloned.1.call-start
  6.5 0.7 compare_select_fusion
  7.3 0.1 copy.22
  7.3 0.1 reshape.66
  7.5 1.3 reshape.60
  8.8 0.2 copy.23
  9.0 0.7 iota_compare_fusion.2
  9.7 0.0 copy-done.1
  9.7 1.6 gather_fusion.1
  11.2 0.0 copy-start.4
  11.3 1.0 gather_fusion
  12.3 0.1 reshape.73
  12.4 0.1 iota_compare_fusion
  12.5 0.0 copy-done.4
  12.5 0.1 iota_compare_fusion.1
  12.6 34.4 %reshape_squeeze.3 = bf16[8,32,6,64,64]{4,3,1,2,0:T(8,128)(2,1)} reshape(bf16[1,8,32,6,4096]{4,2,3,1,0:T(8,128)(2,1)} %param.6) | data formatting | bytes 25165824 | tf_op jit(solution)/shard_map/reshape;squeeze | solution.py:35
  47.0 2.3 and_and_fusion
  49.3 17.0 %fusion.5 = bf16[8,32,64,48]{2,3,0,1:T(8,128)(2,1)} fusion(bf16[32,6,64,48,1]{2,3,1,4,0:T(8,128)(2,1)S(1)} %bitcast.46, bf16[8,32,6,64,64]{4,3,1,2,0:T(8,128)(2,1)} %reshape_squeeze.3, pred[32,6,64,64]{3,2,1,0:T(8,128)(4,1)} %and_and_fusion), kind=kOutput, calls=%fused_computation.11 | convolution fusion | flops 611057664 | bytes 16121856 | tf_op jit(solution)/shard_map/qmkab,mkbi->qmai/dot_general | solution.py:38
  66.3 6.2 %copy.33 = bf16[8,32,64,48]{3,2,0,1:T(8,128)(2,1)} copy(bf16[8,32,64,48]{2,3,0,1:T(8,128)(2,1)} %fusion.5) | data formatting | bytes 3145728 | tf_op jit(solution)/shard_map/reshape | solution.py:41
  72.5 8.0 %reshape.87 = bf16[8,32,3072]{2,0,1:T(8,128)(2,1)S(1)} reshape(bf16[8,32,64,48]{3,2,0,1:T(8,128)(2,1)} %copy.33) | data formatting | bytes 3145728 | tf_op jit(solution)/shard_map/reshape | solution.py:41
  80.5 44.1 %all_to_all.15 = bf16[8,32,3072]{2,0,1:T(8,128)(2,1)S(1)} all-to-all(bf16[8,32,3072]{2,0,1:T(8,128)(2,1)S(1)} %reshape.87), channel_id=1, replica_groups=mesh['grp'=8,'rep'=4] {'grp'}, dimensions={1} | all-to-all | bytes 3145728 | tf_op jit(solution)/shard_map/all_to_all | solution.py:42
  124.5 0.1 copy.40
  124.6 5.3 reshape.62
  130.0 6.4 %copy.28 = bf16[64,4,64,48]{0,2,3,1:T(8,128)(2,1)S(1)} copy(bf16[64,4,64,48]{3,2,0,1:T(8,128)(2,1)} %reshape.62) | data formatting | bytes 3145728 | tf_op jit(solution)/shard_map/reshape | solution.py:45
  136.4 0.0 copy-done
  136.4 2.6 convert_bitcast_fusion
  139.0 7.3 %copy.29 = bf16[4,64,64,48]{1,0,3,2:T(4,128)(2,1)} copy(bf16[4,64,64,48]{2,1,3,0:T(8,128)(2,1)} %convert_bitcast_fusion) | data formatting | bytes 3145728 | tf_op jit(solution)/shard_map/convert_element_type | solution.py:48
  146.3 4.8 reshape.63
  151.1 2.4 collective-permute-start
  153.5 33.3 %collective-permute-done = bf16[256,3072]{0,1:T(8,128)(2,1)S(1)} collective-permute-done((bf16[256,3072]{0,1:T(8,128)(2,1)S(1)}, bf16[256,3072]{0,1:T(8,128)(2,1)S(1)}, u32[]{:S(2)}, u32[]{:S(2)}) %collective-permute-start) | collective-permute-done | bytes 1572896 | tf_op jit(solution)/shard_map/ppermute | solution.py:20
  186.8 0.2 pad_maximum_fusion.1
  187.0 1.4 collective-permute-start.1
  188.4 67.3 %collective-permute-done.1 = bf16[512,3072]{0,1:T(8,128)(2,1)S(1)} collective-permute-done((bf16[512,3072]{0,1:T(8,128)(2,1)S(1)}, bf16[512,3072]{0,1:T(8,128)(2,1)S(1)}, u32[]{:S(2)}, u32[]{:S(2)}) %collective-permute-start.1) | collective-permute-done | bytes 3145760 | tf_op jit(solution)/shard_map/ppermute | solution.py:20
  255.7 0.0 copy-start.2
  255.7 3.6 pad_maximum_fusion
  259.3 0.0 copy-done.2
  259.3 0.3 collective-permute-start.2
  259.5 0.0 copy-start.3
  259.6 1.3 constant_dynamic-update-slice_fusion.7
  260.8 1.3 constant_dynamic-update-slice_fusion.6
  262.1 0.2 copy-done.3
  262.3 1.9 constant_dynamic-update-slice_fusion.5
  264.2 266.1 %collective-permute-done.2 = bf16[1024,3072]{0,1:T(8,128)(2,1)} collective-permute-done((bf16[1024,3072]{0,1:T(8,128)(2,1)}, bf16[1024,3072]{0,1:T(8,128)(2,1)}, u32[]{:S(2)}, u32[]{:S(2)}) %collective-permute-start.2) | collective-permute-done | bytes 6291488 | tf_op jit(solution)/shard_map/ppermute | solution.py:20
  530.3 6.1 %constant_dynamic-update-slice_fusion.4 = bf16[4096,3072]{0,1:T(8,128)(2,1)} fusion(bf16[4096,3072]{0,1:T(8,128)(2,1)} %constant_dynamic-update-slice_fusion.5, bf16[1024,3072]{0,1:T(8,128)(2,1)} %collective-permute-done.2), kind=kLoop, calls=%fused_computation.20 | loop fusion | bytes 12582912
  536.5 1.3 constant_dynamic-update-slice_fusion.3
  537.8 1.3 constant_dynamic-update-slice_fusion.2
  539.1 1.9 constant_dynamic-update-slice_fusion.1
  541.1 6.2 %constant_dynamic-update-slice_fusion = bf16[4096,3072]{0,1:T(8,128)(2,1)} fusion(bf16[4096,3072]{0,1:T(8,128)(2,1)} %constant_dynamic-update-slice_fusion.1, bf16[1024,3072]{0,1:T(8,128)(2,1)} %collective-permute-done.2), kind=kLoop, calls=%fused_computation.16 | loop fusion | bytes 12582912 | tf_op jit(solution)/shard_map/jit(_roll_dynamic)/concatenate | solution.py:22
  547.2 8.0 %fusion.2 = f32[2048,256]{1,0:T(8,128)} fusion(bf16[256,3072]{0,1:T(8,128)(2,1)S(1)} %reshape.63, bf16[4096,3072]{0,1:T(8,128)(2,1)} %constant_dynamic-update-slice_fusion, s32[]{:T(128)S(6)} %select_n.24), kind=kOutput, calls=%fused_computation.5 | convolution fusion | flops 3221225472 | bytes 16252932 | tf_op jit(solution)/shard_map/dot_general | solution.py:50
  555.2 0.0 reduce-scatter.2.cloned.1.call-update
  555.2 33.5 %reduce-scatter.2.cloned.1.call-done = f32[512,256]{1,0:T(8,128)} async-done(((f32[2048,256]{1,0:T(8,128)}), f32[512,256]{1,0:T(8,128)}) %reduce-scatter.2.cloned.1.call-update) | async-done | bytes 524304 | tf_op jit(solution)/shard_map/reduce_scatter | solution.py:51
  (1 shorter events, 0.0 us)
Async XLA Ops:
  6.5 129.9 %copy-start = (bf16[1,64,64]{2,1,0:T(8,128)(2,1)S(1)}, bf16[1,64,64]{2,1,0:T(8,128)(2,1)}, u32[]{:S(2)}) copy-start(bf16[1,64,64]{2,1,0:T(8,128)(2,1)} %param.7) | copy-start | bytes 24580
  6.5 3.2 copy-start.1
  6.5 582.2 %reduce-scatter.2.cloned.1.call-start = ((), (), s32[]{:S(2)}) async-start(), calls=%async_computation.2 | async-start | bytes 2621440 | tf_op jit(solution)/shard_map/reduce_scatter | solution.py:51
  11.2 1.3 copy-start.4
  151.1 35.7 %collective-permute-start = (bf16[256,3072]{0,1:T(8,128)(2,1)S(1)}, bf16[256,3072]{0,1:T(8,128)(2,1)S(1)}, u32[]{:S(2)}, u32[]{:S(2)}) collective-permute-start(bf16[256,3072]{0,1:T(8,128)(2,1)S(1)} %reshape.63), channel_id=1, source_target_pairs={{0,28},{4,0},{8,4},{12,8},{16,12},{20,16},{24,20},{28,24},{1,29},{... | collective-permute-start | bytes 4718600 | tf_op jit(solution)/shard_map/ppermute | solution.py:20
  187.0 68.6 %collective-permute-start.1 = (bf16[512,3072]{0,1:T(8,128)(2,1)S(1)}, bf16[512,3072]{0,1:T(8,128)(2,1)S(1)}, u32[]{:S(2)}, u32[]{:S(2)}) collective-permute-start(bf16[512,3072]{0,1:T(8,128)(2,1)S(1)} %pad_maximum_fusion.1), channel_id=1, source_target_pairs={{0,24},{4,28},{8,0},{12,4},{16,8},{20,12},{24,16},{28,20},{1,25},{... | collective-permute-start | bytes 9437192 | tf_op jit(solution)/shard_map/ppermute | solution.py:20
  255.7 3.6 copy-start.2
  259.3 271.1 %collective-permute-start.2 = (bf16[1024,3072]{0,1:T(8,128)(2,1)}, bf16[1024,3072]{0,1:T(8,128)(2,1)}, u32[]{:S(2)}, u32[]{:S(2)}) collective-permute-start(bf16[1024,3072]{0,1:T(8,128)(2,1)} %pad_maximum_fusion), channel_id=1, source_target_pairs={{0,16},{4,20},{8,24},{12,28},{16,0},{20,4},{24,8},{28,12},{1,17},{... | collective-permute-start | bytes 18874376 | tf_op jit(solution)/shard_map/ppermute | solution.py:20
  259.5 2.7 copy-start.3
Sparse Core Ops, SparseCore 0:
  555.3 33.3 reduce-scatter.1
